TPU v7x, 512 devices: a whole 4x4x16 slice. The times are simulated.
512 devices in a mesh: col: 32 (over y, x, core), row: 16 (over z).
Axes of the slice: x: 4, y: 4, z: 16, core: 2. Of those that a mesh axis runs over, the one named last changes fastest.
Arguments:
- normal_matrix: float32 [4, 16, 128, 2, 32, 128], P(None, 'row', None, None, 'col'), may hold values from -3 to 5.5, as said below
- right_sides: float32 [256, 4, 16, 128], P('col', None, 'row'), may hold values from -6 to 6
Outputs:
- reduced_matrix: float32 [4, 16, 128, 2, 32, 128], P(None, 'row', None, None, 'col')
- reduced_sides: float32 [256, 4, 16, 128], P('col', None, 'row')
Inputs may be any that keep to these rules, and one draw needn't show every extreme that they name: `normal_matrix`: A is symmetric; its leading 128 x 128 block is strictly diagonally dominant with a positive diagonal.
All inputs are finite; a program needn't handle non-finite values.
Results may differ from a plain program's by a relative error of at most 0.00005.
Values sent between devices are 32-bit elements; how exact they have to be, the bound alone decides.
No kernel may reach another device: no remote copies, remote signals or barrier semaphores. Data moves between devices by JAX's collectives and lax.ppermute only.
A program may use at most 64 MiB of HBM per device.

v0:
```python
import jax
import jax.numpy as jnp
from jax import lax
from jax.sharding import PartitionSpec as P


def spread(block, axis, holder):
    block = jnp.where(lax.axis_index(axis) == holder, block, jnp.zeros_like(block))
    return lax.psum(block, axis)


def on_device(normal_matrix, right_sides):
    row_blocks, _, block, col_blocks, _, _ = normal_matrix.shape
    col_id = lax.axis_index("col")
    row_id = lax.axis_index("row")
    col_count = lax.axis_size("col")
    row_count = lax.axis_size("row")
    local = normal_matrix.reshape(row_blocks * block, col_blocks * block)
    first = local[:, :block]
    corner_raw = spread(first[:block], "row", 0)
    identity = jnp.eye(block, dtype=jnp.float32)
    corner_raw = jnp.where(col_id == 0, corner_raw, identity)
    corner_own = jnp.linalg.cholesky(corner_raw)
    rows_own = jax.scipy.linalg.solve_triangular(corner_own, first.T, lower=True).T
    stacked = jnp.concatenate([corner_own, rows_own], axis=0)
    stacked = spread(stacked, "col", 0)
    corner = stacked[:block]
    rows_factor = stacked[block:]
    picked = []
    for index in range(col_blocks):
        start = (index * col_count + col_id) // row_count * block
        picked.append(lax.dynamic_slice_in_dim(rows_factor, start, block, 0))
    selected = jnp.concatenate(picked, axis=0)
    cols_factor = spread(selected, "row", col_id % row_count)
    change = jnp.dot(
        rows_factor,
        cols_factor.T,
        precision=lax.Precision.HIGHEST,
        preferred_element_type=jnp.float32,
    )
    trailing = (local - change).reshape(row_blocks, block, col_blocks, block)
    global_rows = row_id + row_count * jnp.arange(row_blocks, dtype=jnp.int32)
    global_cols = col_id + col_count * jnp.arange(col_blocks, dtype=jnp.int32)
    inner = (global_rows[:, None, None, None] >= 1) & (global_cols[None, None, :, None] >= 1)
    result = jnp.where(inner, trailing, jnp.float32(0.0))
    column = jnp.where(
        global_rows[:, None, None] == 0, corner[None], rows_factor.reshape(row_blocks, block, block)
    )
    result = jnp.where((global_cols == 0)[None, None, :, None], column[:, :, None, :], result)
    result = result.reshape(normal_matrix.shape)
    side_count = right_sides.shape[0]
    top_sides = spread(right_sides[:, 0, 0, :], "row", 0)
    lead = jax.scipy.linalg.solve_triangular(corner, top_sides.T, lower=True).T
    flat = right_sides.reshape(side_count, row_blocks * block)
    reduced = flat - jnp.dot(
        lead, rows_factor.T, precision=lax.Precision.HIGHEST, preferred_element_type=jnp.float32
    )
    reduced = reduced.reshape(side_count, row_blocks, block)
    reduced = jnp.where((global_rows == 0)[None, :, None], lead[:, None, :], reduced)
    return (result, reduced.reshape(right_sides.shape))


def solution(mesh):
    placed = (P(None, "row", None, None, "col", None), P("col", None, "row", None))
    return jax.shard_map(
        on_device,
        mesh=mesh,
        in_specs=placed,
        out_specs=(P(None, "row", None, None, "col", None), P("col", None, "row", None)),
        check_vma=False,
    )
```

profile of v0, /device:TPU:2, one launch (start us, length us, event | category | flops | bytes accessed | tf_op | source)
XLA Modules:
  0.0 458.6 jit_solution(13755997180216444617)
XLA Ops:
  7.2 1.1 copy.16
  8.3 0.6 slice_select_fusion
  9.0 0.6 copy-done.3
  9.7 139.2 %all-reduce.4.cloned.1.call-done = f32[128,128]{1,0:T(8,128)} async-done(((f32[128,128]{1,0:T(8,128)}), f32[128,128]{1,0:T(8,128)}) %all-reduce.4.cloned.1.call-update) | async-done | bytes 65552 | tf_op jit(solution)/shard_map/psum | solution.py:9
  149.1 0.7 copy-done.2
  149.9 11.7 %cholesky.19 = f32[128,128]{1,0:T(8,128)S(1)} custom-call(f32[128,128]{1,0:T(8,128)S(1)} %fusion.5), custom_call_target="Cholesky" | custom-call | tf_op jit(solution)/shard_map/jit(cholesky)/cholesky | solution.py:23
  161.6 0.6 compare_reduce_fusion
  162.2 0.7 select_bitcast_fusion.1
  162.9 9.8 %custom-call.11 = f32[1,128,128]{1,2,0:T(8,128)S(1)} custom-call(f32[1,128,128]{2,1,0:T(8,128)S(1)} %get-tuple-element.2), custom_call_target="InvertDiagBlocksLowerTriangular" | custom-call | tf_op jit(solution)/shard_map/jit(_solve_triangular)/triangular_solve | solution.py:24
  172.7 0.4 convolution_bitcast_fusion
  173.1 0.7 maximum_select_fusion
  174.0 27.5 %psum.31 = f32[8,128]{1,0:T(8,128)S(1)} all-reduce(f32[8,128]{1,0:T(8,128)S(1)} %bitcast.46), channel_id=1, replica_groups=mesh['col'=32,'row'=16] {'row'}, use_global_device_ids=true, to_apply=%region_5.6 | all-reduce | flops 1024 | bytes 8192 | tf_op jit(solution)/shard_map/psum | solution.py:9
  201.5 100.2 %all-reduce.6.cloned.1.call-done = f32[640,128]{1,0:T(8,128)} async-done(((f32[640,128]{1,0:T(8,128)}), f32[640,128]{1,0:T(8,128)}) %all-reduce.6.cloned.1.call-update) | async-done | bytes 327696 | tf_op jit(solution)/shard_map/psum | solution.py:9
  301.7 0.8 select_bitcast_fusion
  302.5 9.8 %custom-call.12 = f32[1,128,128]{1,2,0:T(8,128)S(1)} custom-call(f32[1,128,128]{2,1,0:T(8,128)S(1)} %get-tuple-element.4), custom_call_target="InvertDiagBlocksLowerTriangular" | custom-call | tf_op jit(solution)/shard_map/jit(_solve_triangular)/triangular_solve | solution.py:53
  312.4 1.0 slice.42
  313.4 0.7 maximum_select_fusion.1
  314.3 0.7 copy-done
  315.0 0.3 fusion
  315.3 0.7 broadcast_select_fusion.3
  316.0 132.8 %all-reduce.8.cloned.1.call-done = f32[256,128]{1,0:T(8,128)} async-done(((f32[256,128]{1,0:T(8,128)}), f32[256,128]{1,0:T(8,128)}) %all-reduce.8.cloned.1.call-update) | async-done | bytes 131088 | tf_op jit(solution)/shard_map/psum | solution.py:9
  448.8 1.5 convolution_subtract_fusion
  450.3 0.3 reshape.136
  450.6 1.5 broadcast_select_fusion
  (24 shorter events, 0.7 us)
Async XLA Ops:
  7.2 141.8 %all-reduce.4.cloned.1.call-start = ((), (), s32[]{:S(2)}) async-start(), calls=%async_computation | async-start | bytes 131072 | tf_op jit(solution)/shard_map/psum | solution.py:9
  8.9 0.7 copy-start.3
  9.0 292.7 %all-reduce.6.cloned.1.call-start = ((), (), s32[]{:S(2)}) async-start(), calls=%async_computation.1 | async-start | bytes 655360 | tf_op jit(solution)/shard_map/psum | solution.py:9
  149.0 0.8 copy-start.2
  173.9 274.9 %all-reduce.8.cloned.1.call-start = ((), (), s32[]{:S(2)}) async-start(), calls=%async_computation.2 | async-start | bytes 262144 | tf_op jit(solution)/shard_map/psum | solution.py:9
  314.0 1.0 copy-start
  314.1 134.7 %copy-start.1 = (f32[4,1,128,2,1,128]{5,4,3,2,1,0:T(1,128)S(1)}, f32[4,1,128,2,1,128]{5,4,3,2,1,0:T(1,128)}, u32[]{:S(2)}) copy-start(f32[4,1,128,2,1,128]{5,4,3,2,1,0:T(1,128)} %param.2) | copy-start | bytes 1572868
Sparse Core Ops, SparseCore 0:
  10.9 138.0 all-reduce.3
  174.0 127.6 all-reduce.5
  314.2 134.5 all-reduce.7
where the time goes:
time: 459 us
  waiting for transfers between devices  372 us (81%)
  other arithmetic  38 us (8%)
  blocking collectives  27.5 us (6%)
  between operations  13.9 us (3%)
    psum x3, waiting for transfers between devices, spread(): return lax.psum(block, axis)  372 us
    psum x1, blocking collectives, spread(): return lax.psum(block, axis)  27.5 us
    another operation x3, other arithmetic, on_device(): corner_own = jnp.linalg.cholesky(corner_raw)  12.4 us
    another operation x2, other arithmetic, on_device(): lead = jax.scipy.linalg.solve_triangular(corner, top_sides.T, lower=True).T  10.7 us
    another operation x2, other arithmetic, on_device(): jax.scipy.linalg.solve_triangular(corner_own, first.T, lower=True)  10.5 us
  transfers between devices with their start and end apart: 3, of which 3 were waited for; matrix products, arithmetic and copies ran while one was open for 0% of the time, Pallas kernels for 0%

commit v1 on v0

--- a/solution.py
+++ b/solution.py
@@ -4,9 +4,15 @@
 from jax.sharding import PartitionSpec as P
 
 
+def cover_vector(obj, mesh_ax):
+    spare = jax.lax.all_gather(obj, axis_name=mesh_ax)
+    carry_in = jnp.sum(spare, 0)
+    return carry_in
+
+
 def spread(block, axis, holder):
     block = jnp.where(lax.axis_index(axis) == holder, block, jnp.zeros_like(block))
-    return lax.psum(block, axis)
+    return cover_vector(block, mesh_ax=axis)
 
 
 def on_device(normal_matrix, right_sides):

time: 459 us -> 272 us (0.59)
  waiting for transfers between devices: 372 us -> 179 us
  other arithmetic: 38 us -> 44 us
    psum x3 -> x0, waiting for transfers between devices: 372 us -> none  [spread(): return lax.psum(block, axis)]
    all_gather x0 -> x3, waiting for transfers between devices: none -> 178 us  [cover_vector(): spare = jax.lax.all_gather(obj, axis_name=mesh_ax)]
    all_gather x0 -> x1, blocking collectives: none -> 30.7 us  [cover_vector(): spare = jax.lax.all_gather(obj, axis_name=mesh_ax)]
    psum x1 -> x0, blocking collectives: 27.5 us -> none  [spread(): return lax.psum(block, axis)]
    reduce_sum x0 -> x4, other arithmetic: none -> 7.48 us  [cover_vector(): carry_in = jnp.sum(spare, 0)]
    another operation x2 -> x1, other arithmetic: 10.5 us -> 9.81 us  [on_device(): jax.scipy.linalg.solve_triangular(corner_own, first.T, lower=True)]
  transfers between devices with their start and end apart: 3 -> 3, of which waited for: 3 -> 3; matrix products, arithmetic and copies ran while one was open for 0% -> 4% of each run, Pallas kernels for 0% -> 0%
where the time goes in v1:
time: 272 us
  waiting for transfers between devices  179 us (66%)
  other arithmetic  44 us (16%)
  blocking collectives  30.7 us (11%)
  between operations  14 us (5%)
  local copies, waits for them, and re-layouts  3.09 us (1%)
    all_gather x3, waiting for transfers between devices, cover_vector(): spare = jax.lax.all_gather(obj, axis_name=mesh_ax)  178 us
    all_gather x1, blocking collectives, cover_vector(): spare = jax.lax.all_gather(obj, axis_name=mesh_ax)  30.7 us
    another operation x3, other arithmetic, on_device(): corner_own = jnp.linalg.cholesky(corner_raw)  12.4 us
    another operation x2, other arithmetic, on_device(): lead = jax.scipy.linalg.solve_triangular(corner, top_sides.T, lower=True).T  9.82 us
    another operation x1, other arithmetic, on_device(): jax.scipy.linalg.solve_triangular(corner_own, first.T, lower=True)  9.81 us
    reduce_sum x4, other arithmetic, cover_vector(): carry_in = jnp.sum(spare, 0)  7.48 us
  transfers between devices with their start and end apart: 3, of which 3 were waited for; matrix products, arithmetic and copies ran while one was open for 4% of the time, Pallas kernels for 0%

profile of v1, /device:TPU:2, one launch (start us, length us, event | category | flops | bytes accessed | tf_op | source)
XLA Modules:
  0.0 271.9 jit_solution(14735918429483486960)
XLA Ops:
  7.2 1.1 copy.39
  8.3 0.6 slice_select_fusion
  9.0 77.1 %all-gather.10.cloned.1.call-done = f32[2048,128]{1,0:T(8,128)} async-done(((f32[128,128]{1,0:T(8,128)}), f32[2048,128]{1,0:T(8,128)}) %all-gather.10.cloned.1.call-update) | async-done | bytes 1048592 | tf_op jit(solution)/shard_map/all_gather | solution.py:8
  86.2 1.3 reduce_sum.38
  87.6 11.7 %cholesky.19 = f32[128,128]{1,0:T(8,128)S(1)} custom-call(f32[128,128]{1,0:T(8,128)S(1)} %fusion.6), custom_call_target="Cholesky" | custom-call | tf_op jit(solution)/shard_map/jit(cholesky)/cholesky | solution.py:29
  99.3 0.6 compare_reduce_fusion
  100.0 0.7 fusion.7
  100.7 9.8 %custom-call.11 = f32[1,128,128]{1,2,0:T(8,128)S(1)} custom-call(f32[1,128,128]{2,1,0:T(8,128)S(1)} %get-tuple-element.7), custom_call_target="InvertDiagBlocksLowerTriangular" | custom-call | tf_op jit(solution)/shard_map/jit(_solve_triangular)/triangular_solve | solution.py:30
  110.5 0.4 convolution_bitcast_fusion
  111.0 0.9 copy.19
  112.0 70.1 %all-gather.6.cloned.1.call-done = f32[32,640,128]{2,1,0:T(8,128)} async-done(((f32[1,640,128]{2,1,0:T(8,128)}), f32[32,640,128]{2,1,0:T(8,128)}) %all-gather.6.cloned.1.call-update) | async-done | bytes 10485776 | tf_op jit(solution)/shard_map/all_gather | solution.py:8
  182.1 4.5 %reduce_sum.40 = f32[640,128]{1,0:T(8,128)S(1)} reduce(f32[32,640,128]{2,1,0:T(8,128)} %all-gather.6.cloned.1.call-done, f32[]{:T(128)} %constant.100.clone.1), dimensions={0}, to_apply=%region_3.4 | reduce | flops 2539520 | bytes 10813444 | tf_op jit(solution)/shard_map/reduce_sum | solution.py:9
  187.0 0.7 maximum_select_fusion.1
  187.7 30.7 %all-gather.1 = f32[128,1,1,128]{3,2,1,0:T(1,128)S(1)} all-gather(f32[8,1,1,128]{3,2,1,0:T(1,128)S(1)} %broadcast_select_fusion.4), channel_id=3, replica_groups=mesh['col'=32,'row'=16] {'row'}, dimensions={0}, use_global_device_ids=true | all-gather | bytes 69632 | tf_op jit(solution)/shard_map/all_gather | solution.py:8
  218.7 9.8 %custom-call.12 = f32[1,128,128]{1,2,0:T(8,128)S(1)} custom-call(f32[1,128,128]{2,1,0:T(8,128)S(1)} %get-tuple-element.2), custom_call_target="InvertDiagBlocksLowerTriangular" | custom-call | tf_op jit(solution)/shard_map/jit(_solve_triangular)/triangular_solve | solution.py:59
  228.6 0.1 broadcast_select_fusion.2
  228.9 0.2 fusion.2
  229.0 0.3 fusion
  229.4 0.7 broadcast_select_fusion.3
  230.1 31.2 %all-gather.8.cloned.1.call-done = f32[16,256,128]{2,1,0:T(8,128)} async-done(((f32[1,256,128]{2,1,0:T(8,128)}), f32[16,256,128]{2,1,0:T(8,128)}) %all-gather.8.cloned.1.call-update) | async-done | bytes 2097168 | tf_op jit(solution)/shard_map/all_gather | solution.py:8
  261.3 1.7 reduce_sum.41
  263.0 0.6 convolution_subtract_fusion
  263.6 0.3 reshape.204
  263.9 1.5 broadcast_select_fusion
  (31 shorter events, 1.3 us)
Async XLA Ops:
  7.2 180.6 %copy-start.1 = (f32[8,4,1,128]{3,2,1,0:T(1,128)S(1)}, f32[8,4,1,128]{3,2,1,0:T(1,128)}, u32[]{:S(2)}) copy-start(f32[8,4,1,128]{3,2,1,0:T(1,128)} %param.3) | copy-start | bytes 49156
  7.2 79.0 %all-gather.10.cloned.1.call-start = ((), (), s32[]{:S(2)}) async-start(), calls=%async_computation.2 | async-start | bytes 1114112 | tf_op jit(solution)/shard_map/all_gather | solution.py:8
  9.0 173.2 %all-gather.6.cloned.1.call-start = ((), (), s32[]{:S(2)}) async-start(), calls=%async_computation | async-start | bytes 10813440 | tf_op jit(solution)/shard_map/all_gather | solution.py:8
  87.5 175.5 %copy-start = (f32[4,1,128,2,1,128]{5,4,3,2,1,0:T(1,128)S(1)}, f32[4,1,128,2,1,128]{5,4,3,2,1,0:T(1,128)}, u32[]{:S(2)}) copy-start(f32[4,1,128,2,1,128]{5,4,3,2,1,0:T(1,128)} %param.2) | copy-start | bytes 1572868
  111.9 149.3 %all-gather.8.cloned.1.call-start = ((), (), s32[]{:S(2)}) async-start(), calls=%async_computation.1 | async-start | bytes 2228224 | tf_op jit(solution)/shard_map/all_gather | solution.py:8
Sparse Core Ops, SparseCore 0:
  10.7 75.4 all-gather.9
  112.1 70.0 all-gather.5
  187.8 73.3 all-gather.7
